TPU v7x, 32 devices: a whole 2x2x4 slice. The times are simulated.
32 devices in a mesh: gx: 8 (over z, y), gy: 4 (over x, core).
Axes of the slice: x: 2, y: 2, z: 4, core: 2. Of those that a mesh axis runs over, the one named last changes fastest.
Arguments:
- conc_prev: float32 [128, 64, 128], P('gx', 'gy'), may hold values from 0.5 to 2
- right_side: float32 [128, 64, 128], P('gx', 'gy'), may hold values from -5 to 7
- soil_id: int32 [128, 64, 128], P('gx', 'gy'), may hold values from 0 to 7
- soil_table: float32 [5, 8], replicated, may hold values from 0.3 to 3
Outputs:
- correction: float32 [128, 64, 128], P('gx', 'gy')
All inputs are finite; a program needn't handle non-finite values.
Results may differ from a plain program's by a relative error of at most 0.00002.
Values sent between devices are 32-bit elements; how exact they have to be, the bound alone decides.
No kernel may reach another device: no remote copies, remote signals or barrier semaphores. Data moves between devices by JAX's collectives and lax.ppermute only.
A program may use at most 128 MiB of HBM per device.

v0:
```python
import jax
import jax.numpy as jnp
from jax import lax
from jax.sharding import PartitionSpec as P

CHEB = 3
COARSE_SWEEPS = 8
storage_scale = 0.05
cheb_centre = 1.1
cheb_half = 0.9
cheb_ratio = cheb_centre / cheb_half
jacobi_weight = 0.8


def padded_2(cells, sides, width):
    for axis, dim in sides:
        count = lax.axis_size(axis)
        ends = count - 1
        head = lax.slice_in_dim(cells, 0, width, axis=dim)
        tail = lax.slice_in_dim(cells, cells.shape[dim] - width, cells.shape[dim], axis=dim)
        cells = jnp.concatenate(
            [
                lax.ppermute(tail, axis, [(i, (i + 1) % count) for i in range(ends)]),
                cells,
                lax.ppermute(head, axis, [((i + 1) % count, i) for i in range(ends)]),
            ],
            axis=dim,
        )
    return cells


def harmonic(first, second):
    return first * second / jnp.maximum(0.5 * (first + second), 0.1)


def face_terms(coeffs, spacing):
    eastward = coeffs[0]
    northward = coeffs[1]
    upward = coeffs[2]
    centre_x = eastward[1:-1, 1:-1]
    centre_y = northward[1:-1, 1:-1]
    centre_z = upward[1:-1, 1:-1]
    east_face = harmonic(eastward[2:, 1:-1], centre_x) * spacing
    west_face = harmonic(eastward[:-2, 1:-1], centre_x) * spacing
    north_face = harmonic(northward[1:-1, 2:], centre_y) * spacing
    south_face = harmonic(northward[1:-1, :-2], centre_y) * spacing
    vertical = harmonic(centre_z[:, :, 1:], centre_z[:, :, :-1]) * spacing
    closed = jnp.zeros_like(centre_z[:, :, :1])
    above_face = jnp.concatenate([vertical, closed], axis=2)
    below_face = jnp.concatenate([closed, vertical], axis=2)
    storage = coeffs[3, 1:-1, 1:-1]
    return (east_face, west_face, north_face, south_face, above_face, below_face, storage)


def main_diagonal(coeffs, spacing):
    east_face, west_face, north_face, south_face, above_face, below_face, storage = face_terms(
        coeffs, spacing
    )
    return jnp.maximum(
        storage + east_face + west_face + north_face + south_face + above_face + below_face, 0.01
    )


def operate(values, coeffs, spacing):
    east_face, west_face, north_face, south_face, above_face, below_face, storage = face_terms(
        coeffs, spacing
    )
    centre = values[1:-1, 1:-1]
    upper_cell = jnp.concatenate([centre[:, :, 1:], centre[:, :, :1]], axis=2)
    lower_cell = jnp.concatenate([centre[:, :, -1:], centre[:, :, :-1]], axis=2)
    fluxes = east_face * (centre - values[2:, 1:-1]) + west_face * (centre - values[:-2, 1:-1])
    fluxes = (
        fluxes
        + north_face * (centre - values[1:-1, 2:])
        + south_face * (centre - values[1:-1, :-2])
    )
    fluxes = fluxes + above_face * (centre - upper_cell) + below_face * (centre - lower_cell)
    return storage * centre + fluxes


def coarsen(values):
    lead = values.shape[:-3]
    size_x, size_y, size_z = values.shape[-3:]
    split = values.reshape(lead + (size_x // 2, 2, size_y // 2, 2, size_z // 2, 2))
    return jnp.mean(split, axis=(-5, -3, -1))


def prolong(values):
    return jnp.repeat(jnp.repeat(jnp.repeat(values, 2, axis=0), 2, axis=1), 2, axis=2)


def shrink(values, amount):
    if amount == 0:
        return values
    return values[..., amount:-amount, amount:-amount, :]


def tile_halo(layers, amount):
    return padded_2(layers, (("gx", 1), ("gy", 2)), amount)


def expand(values):
    return (tile_halo(values[None], 1)[0], 1)


def smooth(target, target_margin, initial, coeffs, coeff_margin, spacing):
    if initial is None:
        current = target_margin
        diagonal = main_diagonal(shrink(coeffs, coeff_margin - current - 1), spacing)
        update = target / diagonal * (1.0 / cheb_centre)
        iterate = update
    else:
        padded, padded_margin = expand(initial)
        applied = operate(padded, shrink(coeffs, coeff_margin - padded_margin), spacing)
        current = padded_margin - 1
        diagonal = main_diagonal(shrink(coeffs, coeff_margin - current - 1), spacing)
        misfit = shrink(target, target_margin - current) - applied
        update = misfit / diagonal * (1.0 / cheb_centre)
        iterate = shrink(padded, 1) + update
    diagonal_margin = current
    factor = 1.0 / cheb_ratio
    for repeat in range(CHEB - 1):
        padded, padded_margin = expand(iterate)
        applied = operate(padded, shrink(coeffs, coeff_margin - padded_margin), spacing)
        next_margin = padded_margin - 1
        misfit = shrink(target, target_margin - next_margin) - applied
        factor_new = 1.0 / (2.0 * cheb_ratio - factor)
        update = factor_new * factor * shrink(
            update, current - next_margin
        ) + 2.0 * factor_new / cheb_half * (
            misfit / shrink(diagonal, diagonal_margin - next_margin)
        )
        iterate = shrink(iterate, current - next_margin) + update
        current = next_margin
        factor = factor_new
    return (iterate, current)


def leftover(target, target_margin, iterate, coeffs, coeff_margin, spacing):
    padded, padded_margin = expand(iterate)
    applied = operate(padded, shrink(coeffs, coeff_margin - padded_margin), spacing)
    return shrink(target, target_margin - padded_margin + 1) - applied


def local_fields(conc_prev, soil_id, soil_table):
    fields = []
    for record in range(5):
        looked = jnp.zeros(soil_id.shape, jnp.float32)
        for material in range(soil_table.shape[1]):
            looked = looked + jnp.where(soil_id == material, soil_table[record, material], 0.0)
        fields.append(looked)
    storage = storage_scale * (1.0 + fields[3] * jnp.exp((fields[4] - 1.0) * jnp.log(conc_prev)))
    return jnp.stack([fields[0], fields[1], fields[2], storage])


def local(conc_prev, right_side, soil_id, soil_table):
    halo_depth = 0
    fine_margin = max(4, 2 * halo_depth + 2)
    own_coeffs = local_fields(conc_prev, soil_id, soil_table)
    fine_coeffs = padded_2(own_coeffs, (("gx", 1), ("gy", 2)), fine_margin)
    mid_margin = fine_margin // 2
    mid_coeffs = coarsen(fine_coeffs)
    coarse_coeffs = coarsen(shrink(mid_coeffs, mid_margin - 2))
    fine_iterate, current = smooth(right_side, halo_depth, None, fine_coeffs, fine_margin, 1.0)
    fine_misfit = leftover(right_side, halo_depth, fine_iterate, fine_coeffs, fine_margin, 1.0)
    fine_iterate = shrink(fine_iterate, current)
    mid_plain = coarsen(fine_misfit)
    mid_iterate, current = smooth(mid_plain, halo_depth, None, mid_coeffs, mid_margin, 0.25)
    mid_misfit = leftover(mid_plain, halo_depth, mid_iterate, mid_coeffs, mid_margin, 0.25)
    mid_iterate = shrink(mid_iterate, current)
    coarse_source = coarsen(mid_misfit)
    narrow = coarse_coeffs[:, :, 1:-1]
    group_source, group_coeffs = (
        lax.all_gather(coarse_source, "gy", axis=1, tiled=True),
        lax.all_gather(narrow, "gy", axis=2, tiled=True),
    )
    line_total = jnp.sum(group_source, axis=1)
    line_store = jnp.sum(group_coeffs[3, 1:-1], axis=1)
    line_mean = line_total / line_store
    group_coeffs = jnp.pad(group_coeffs, ((0, 0), (0, 0), (1, 1), (0, 0)))
    diagonal = main_diagonal(group_coeffs, 0.0625)
    coarse_value = jnp.broadcast_to(line_mean[:, None, :], group_source.shape)
    for sweeps in range(COARSE_SWEEPS):
        padded = padded_2(coarse_value, (("gx", 0),), 1)
        padded = jnp.pad(padded, ((0, 0), (1, 1), (0, 0)))
        applied = operate(padded, group_coeffs, 0.0625)
        coarse_value = coarse_value + jacobi_weight * ((group_source - applied) / diagonal)
    tile_width = coarse_source.shape[1]
    coarse_value = lax.dynamic_slice_in_dim(
        coarse_value, lax.axis_index("gy") * tile_width, tile_width, 1
    )
    mid_start = mid_iterate + prolong(coarse_value)
    mid_result, current = smooth(mid_plain, halo_depth, mid_start, mid_coeffs, mid_margin, 0.25)
    fine_start = fine_iterate + prolong(mid_result)
    fine_result, current = smooth(right_side, halo_depth, fine_start, fine_coeffs, fine_margin, 1.0)
    return fine_result


def solution(mesh):
    placed = (P("gx", "gy", None), P("gx", "gy", None), P("gx", "gy", None), P())
    return jax.shard_map(
        local, mesh=mesh, in_specs=placed, out_specs=P("gx", "gy", None), check_vma=False
    )
```

profile of v0, /device:TPU:26, one launch (start us, length us, event | category | flops | bytes accessed | tf_op | source)
XLA Modules:
  0.0 402.7 jit_solution(15851466285160394497)
XLA Ops:
  5.6 6.3 %add_bitcast_fusion.3 = (f32[1,16,16,128]{3,2,1,0:T(8,128)S(1)}, pred[16,16,128]{2,1,0:T(8,128)(4,1)S(1)}, pred[16,16,128]{2,1,0:T(8,128)(4,1)S(1)}, pred[16,16,...) fusion(f32[]{:T(128)} %bitcast.23, f32[]{:T(128)} %bitcast.22, ...), kind=kLoop, calls=%fused_computation.162 | loop fusion | flops 753664 | bytes 524320 | tf_op jit(solution)/shard_map/stack | solution.py:153
  11.9 5.3 %add_bitcast_fusion.1 = f32[1,16,16,128]{3,2,1,0:T(8,128)S(1)} fusion(pred[16,16,128]{2,1,0:T(8,128)(4,1)S(1)} %get-tuple-element.49, pred[16,16,128]{2,1,0:T(8,128)(4,1)S(1)} %get-tuple-element.48, pred[16,16,128]{2,1,0:T(8,128)(4,1)S(1)} %get-tuple-element.47, pred[16,16,128]{2,1,0:T(8,128)(4,1)S(1)} %get-tuple-element.46, ...), kind=kLoop, calls=%fused_computation.160 | loop fusion | flops 491520 | bytes 393248 | tf_op jit(solution)/shard_map/stack | solution.py:153
  17.2 5.0 %add_bitcast_fusion.2 = f32[1,16,16,128]{3,2,1,0:T(8,128)S(1)} fusion(pred[16,16,128]{2,1,0:T(8,128)(4,1)S(1)} %get-tuple-element.49, pred[16,16,128]{2,1,0:T(8,128)(4,1)S(1)} %get-tuple-element.48, pred[16,16,128]{2,1,0:T(8,128)(4,1)S(1)} %get-tuple-element.47, pred[16,16,128]{2,1,0:T(8,128)(4,1)S(1)} %get-tuple-element.46, ...), kind=kLoop, calls=%fused_computation.161 | loop fusion | flops 491520 | bytes 393248 | tf_op jit(solution)/shard_map/stack | solution.py:153
  22.1 10.1 %add_multiply_fusion = f32[16,16,128]{2,1,0:T(8,128)S(1)} fusion(f32[16,16,128]{2,1,0:T(8,128)S(1)} %copy-done.1, pred[16,16,128]{2,1,0:T(8,128)(4,1)S(1)} %get-tuple-element.49, pred[16,16,128]{2,1,0:T(8,128)(4,1)S(1)} %get-tuple-element.48, pred[16,16,128]{2,1,0:T(8,128)(4,1)S(1)} %get-tuple-element.47, pred[16,16,128]{2,1,0:T(8,128)(4,1)S(1)} %get-tuple-element.46, ...), kind=kLoop, calls=%fused_computation.163 | loop fusion | flops 1146880 | bytes 524352 | tf_op jit(solution)/shard_map/mul | solution.py:152
  39.5 4.0 collective-permute-done
  72.8 3.9 collective-permute-start.8
  76.7 18.2 %copy.868 = f32[4,24,24,128]{0,3,2,1:T(8,128)} copy(f32[4,24,24,128]{3,2,1,0:T(8,128)S(1)} %pad_maximum_fusion) | data formatting | bytes 2359296 | tf_op jit(solution)/shard_map/concatenate | solution.py:21
  94.9 27.0 %reduce_sum.55 = f32[4,12,12,64]{0,3,2,1:T(8,128)} reduce(f32[4,12,2,12,2,64,2]{0,6,5,4,3,2,1:T(2,128)} %bitcast.161, f32[]{:T(128)} %constant.27.clone.1), dimensions={2,4,6}, to_apply=%region_1.2 | reduce | flops 258048 | bytes 1327108 | tf_op jit(solution)/shard_map/reduce_sum | solution.py:85
  149.8 9.8 %reshape.56 = f32[8,2,8,2,64,2]{5,4,3,2,1,0:T(8,128)} reshape(f32[16,16,128]{2,1,0:T(8,128)S(1)} %fusion.41) | data formatting | bytes 262144 | tf_op jit(solution)/shard_map/reshape | solution.py:84
  159.6 4.0 reduce_sum.54
  165.7 4.0 collective-permute-start.16
  172.8 5.3 %reduce_sum.58 = f32[4,6,6,32]{0,3,2,1:T(8,128)S(1)} reduce(f32[4,6,2,6,2,32,2]{0,6,5,4,3,2,1:T(2,128)} %bitcast.162, f32[]{:T(128)} %constant.27.clone.1), dimensions={2,4,6}, to_apply=%region_4.5 | reduce | flops 32256 | bytes 165892 | tf_op jit(solution)/shard_map/reduce_sum | solution.py:85
  191.3 10.7 %all_gather.7 = f32[4,6,16,32]{0,3,2,1:T(8,128)S(1)} all-gather(f32[4,6,4,32]{0,3,2,1:T(8,128)S(1)} %slice_multiply_fusion), channel_id=1, replica_groups=mesh['gx'=8,'gy'=4] {'gy'}, dimensions={2}, use_global_device_ids=true | all-gather | bytes 61440 | tf_op jit(solution)/shard_map/all_gather | solution.py:175
  202.0 4.6 %collective-permute-start.23 = (f32[1,10,1,64]{3,2,1,0:T(1,128)S(1)}, f32[1,10,1,64]{3,2,1,0:T(1,128)S(1)}, u32[]{:S(2)}, u32[]{:S(2)}) collective-permute-start(f32[1,10,1,64]{3,2,1,0:T(1,128)S(1)} %get-tuple-element.143), channel_id=1, source_target_pairs={{1,0},{2,1},{3,2},{5,4},{6,5},{7,6},{9,8},{10,9},{11,10},{13,12},{... | collective-permute-start | bytes 7688 | tf_op jit(solution)/shard_map/ppermute | solution.py:25
  217.9 4.3 %collective-permute-done.24 = f32[1,1,8,64]{3,2,1,0:T(8,128)S(1)} collective-permute-done((f32[1,1,8,64]{3,2,1,0:T(8,128)S(1)}, f32[1,1,8,64]{3,2,1,0:T(8,128)S(1)}, u32[]{:S(2)}, u32[]{:S(2)}) %collective-permute-start.24) | collective-permute-done | bytes 2080 | tf_op jit(solution)/shard_map/ppermute | solution.py:23
  230.6 5.2 %all_gather.6 = f32[4,16,32]{2,0,1:T(4,128)S(1)} all-gather(f32[4,4,32]{2,0,1:T(4,128)S(1)} %copy.879), channel_id=1, replica_groups=mesh['gx'=8,'gy'=4] {'gy'}, dimensions={1}, use_global_device_ids=true | all-gather | bytes 10240 | tf_op jit(solution)/shard_map/all_gather | solution.py:174
  237.9 3.9 collective-permute-start.29
  256.2 3.9 collective-permute-start.33
  274.2 3.9 collective-permute-start.37
  300.1 3.9 collective-permute-start.43
  309.0 3.9 collective-permute-start.44
  324.5 3.9 collective-permute-start.48
  356.6 3.9 collective-permute-start.56
  372.4 3.9 collective-permute-start.60
  (303 shorter events, 242.2 us)
Async XLA Ops:
  32.3 7.1 %collective-permute-start.1 = (f32[4,4,16,128]{3,2,1,0:T(8,128)S(1)}, f32[4,4,16,128]{3,2,1,0:T(8,128)S(1)}, u32[]{:S(2)}, u32[]{:S(2)}) collective-permute-start(f32[4,4,16,128]{3,2,1,0:T(8,128)S(1)} %get-tuple-element.56), channel_id=1, source_target_pairs={{4,0},{8,4},{12,8},{16,12},{20,16},{24,20},{28,24},{5,1},{9,5},{13... | collective-permute-start | bytes 393224 | tf_op jit(solution)/shard_map/ppermute | solution.py:25
  35.6 7.8 %collective-permute-start = (f32[4,4,16,128]{3,2,1,0:T(8,128)S(1)}, f32[4,4,16,128]{3,2,1,0:T(8,128)S(1)}, u32[]{:S(2)}, u32[]{:S(2)}) collective-permute-start(f32[4,4,16,128]{3,2,1,0:T(8,128)S(1)} %get-tuple-element.55), channel_id=1, source_target_pairs={{0,4},{4,8},{8,12},{12,16},{16,20},{20,24},{24,28},{1,5},{5,9},{9,... | collective-permute-start | bytes 393224 | tf_op jit(solution)/shard_map/ppermute | solution.py:23
  45.5 7.0 %collective-permute-start.2 = (f32[4,24,4,128]{3,1,2,0:T(8,128)S(1)}, f32[4,24,4,128]{3,1,2,0:T(8,128)S(1)}, u32[]{:S(2)}, u32[]{:S(2)}) collective-permute-start(f32[4,24,4,128]{3,1,2,0:T(8,128)S(1)} %copy.912), channel_id=1, source_target_pairs={{0,1},{1,2},{2,3},{4,5},{5,6},{6,7},{8,9},{9,10},{10,11},{12,13},{... | collective-permute-start | bytes 589832 | tf_op jit(solution)/shard_map/ppermute | solution.py:23
  57.0 6.4 %collective-permute-start.4 = (f32[1,1,16,128]{3,2,1,0:T(8,128)S(1)}, f32[1,1,16,128]{3,2,1,0:T(8,128)S(1)}, u32[]{:S(2)}, u32[]{:S(2)}) collective-permute-start(f32[1,1,16,128]{3,2,1,0:T(8,128)S(1)} %get-tuple-element.108), channel_id=1, source_target_pairs={{0,4},{4,8},{8,12},{12,16},{16,20},{20,24},{24,28},{1,5},{5,9},{9,... | collective-permute-start | bytes 24584 | tf_op jit(solution)/shard_map/ppermute | solution.py:23
  70.9 54.8 %collective-permute-start.9 = (f32[1,1,16,128]{3,2,1,0:T(8,128)S(1)}, f32[1,1,16,128]{3,2,1,0:T(8,128)S(1)}, u32[]{:S(2)}, u32[]{:S(2)}) collective-permute-start(f32[1,1,16,128]{3,2,1,0:T(8,128)S(1)} %get-tuple-element.107), channel_id=1, source_target_pairs={{4,0},{8,4},{12,8},{16,12},{20,16},{24,20},{28,24},{5,1},{9,5},{13... | collective-permute-start | bytes 24584 | tf_op jit(solution)/shard_map/ppermute | solution.py:25
  72.8 52.9 %collective-permute-start.8 = (f32[1,1,16,128]{3,2,1,0:T(8,128)S(1)}, f32[1,1,16,128]{3,2,1,0:T(8,128)S(1)}, u32[]{:S(2)}, u32[]{:S(2)}) collective-permute-start(f32[1,1,16,128]{3,2,1,0:T(8,128)S(1)} %get-tuple-element.106), channel_id=1, source_target_pairs={{0,4},{4,8},{8,12},{12,16},{16,20},{20,24},{24,28},{1,5},{5,9},{9,... | collective-permute-start | bytes 24584 | tf_op jit(solution)/shard_map/ppermute | solution.py:23
  136.0 6.4 %collective-permute-start.12 = (f32[1,1,16,128]{3,2,1,0:T(8,128)S(1)}, f32[1,1,16,128]{3,2,1,0:T(8,128)S(1)}, u32[]{:S(2)}, u32[]{:S(2)}) collective-permute-start(f32[1,1,16,128]{3,2,1,0:T(8,128)S(1)} %get-tuple-element.104), channel_id=1, source_target_pairs={{0,4},{4,8},{8,12},{12,16},{16,20},{20,24},{24,28},{1,5},{5,9},{9,... | collective-permute-start | bytes 24584 | tf_op jit(solution)/shard_map/ppermute | solution.py:23
  163.7 14.5 %collective-permute-start.17 = (f32[1,1,8,64]{3,2,1,0:T(8,128)S(1)}, f32[1,1,8,64]{3,2,1,0:T(8,128)S(1)}, u32[]{:S(2)}, u32[]{:S(2)}) collective-permute-start(f32[1,1,8,64]{3,2,1,0:T(8,128)S(1)} %get-tuple-element.201), channel_id=1, source_target_pairs={{4,0},{8,4},{12,8},{16,12},{20,16},{24,20},{28,24},{5,1},{9,5},{13... | collective-permute-start | bytes 6152 | tf_op jit(solution)/shard_map/ppermute | solution.py:25
  165.7 12.5 %collective-permute-start.16 = (f32[1,1,8,64]{3,2,1,0:T(8,128)S(1)}, f32[1,1,8,64]{3,2,1,0:T(8,128)S(1)}, u32[]{:S(2)}, u32[]{:S(2)}) collective-permute-start(f32[1,1,8,64]{3,2,1,0:T(8,128)S(1)} %get-tuple-element.200), channel_id=1, source_target_pairs={{0,4},{4,8},{8,12},{12,16},{16,20},{20,24},{24,28},{1,5},{5,9},{9,... | collective-permute-start | bytes 6152 | tf_op jit(solution)/shard_map/ppermute | solution.py:23
  185.5 16.6 %collective-permute-start.21 = (f32[1,1,8,64]{3,2,1,0:T(8,128)S(1)}, f32[1,1,8,64]{3,2,1,0:T(8,128)S(1)}, u32[]{:S(2)}, u32[]{:S(2)}) collective-permute-start(f32[1,1,8,64]{3,2,1,0:T(8,128)S(1)} %get-tuple-element.199), channel_id=1, source_target_pairs={{4,0},{8,4},{12,8},{16,12},{20,16},{24,20},{28,24},{5,1},{9,5},{13... | collective-permute-start | bytes 6152 | tf_op jit(solution)/shard_map/ppermute | solution.py:25
  188.4 13.6 %collective-permute-start.20 = (f32[1,1,8,64]{3,2,1,0:T(8,128)S(1)}, f32[1,1,8,64]{3,2,1,0:T(8,128)S(1)}, u32[]{:S(2)}, u32[]{:S(2)}) collective-permute-start(f32[1,1,8,64]{3,2,1,0:T(8,128)S(1)} %get-tuple-element.198), channel_id=1, source_target_pairs={{0,4},{4,8},{8,12},{12,16},{16,20},{20,24},{24,28},{1,5},{5,9},{9,... | collective-permute-start | bytes 6152 | tf_op jit(solution)/shard_map/ppermute | solution.py:23
  202.0 8.8 %collective-permute-start.23 = (f32[1,10,1,64]{3,2,1,0:T(1,128)S(1)}, f32[1,10,1,64]{3,2,1,0:T(1,128)S(1)}, u32[]{:S(2)}, u32[]{:S(2)}) collective-permute-start(f32[1,10,1,64]{3,2,1,0:T(1,128)S(1)} %get-tuple-element.143), channel_id=1, source_target_pairs={{1,0},{2,1},{3,2},{5,4},{6,5},{7,6},{9,8},{10,9},{11,10},{13,12},{... | collective-permute-start | bytes 7688 | tf_op jit(solution)/shard_map/ppermute | solution.py:25
  215.7 6.4 %collective-permute-start.24 = (f32[1,1,8,64]{3,2,1,0:T(8,128)S(1)}, f32[1,1,8,64]{3,2,1,0:T(8,128)S(1)}, u32[]{:S(2)}, u32[]{:S(2)}) collective-permute-start(f32[1,1,8,64]{3,2,1,0:T(8,128)S(1)} %get-tuple-element.196), channel_id=1, source_target_pairs={{0,4},{4,8},{8,12},{12,16},{16,20},{20,24},{24,28},{1,5},{5,9},{9,... | collective-permute-start | bytes 6152 | tf_op jit(solution)/shard_map/ppermute | solution.py:23
  237.9 6.4 %collective-permute-start.29 = (f32[1,16,32]{2,1,0:T(8,128)S(1)}, f32[1,16,32]{2,1,0:T(8,128)S(1)}, u32[]{:S(2)}, u32[]{:S(2)}) collective-permute-start(f32[1,16,32]{2,1,0:T(8,128)S(1)} %broadcast_in_dim.285), channel_id=1, source_target_pairs={{0,4},{4,8},{8,12},{12,16},{16,20},{20,24},{24,28},{1,5},{5,9},{9,... | collective-permute-start | bytes 6152 | tf_op jit(solution)/shard_map/ppermute | solution.py:23
  247.6 6.4 %collective-permute-start.31 = (f32[1,16,32]{2,1,0:T(8,128)S(1)}, f32[1,16,32]{2,1,0:T(8,128)S(1)}, u32[]{:S(2)}, u32[]{:S(2)}) collective-permute-start(f32[1,16,32]{2,1,0:T(8,128)S(1)} %get-tuple-element.190), channel_id=1, source_target_pairs={{0,4},{4,8},{8,12},{12,16},{16,20},{20,24},{24,28},{1,5},{5,9},{9,... | collective-permute-start | bytes 6152 | tf_op jit(solution)/shard_map/ppermute | solution.py:23
  256.2 6.4 %collective-permute-start.33 = (f32[1,16,32]{2,1,0:T(8,128)S(1)}, f32[1,16,32]{2,1,0:T(8,128)S(1)}, u32[]{:S(2)}, u32[]{:S(2)}) collective-permute-start(f32[1,16,32]{2,1,0:T(8,128)S(1)} %get-tuple-element.184), channel_id=1, source_target_pairs={{0,4},{4,8},{8,12},{12,16},{16,20},{20,24},{24,28},{1,5},{5,9},{9,... | collective-permute-start | bytes 6152 | tf_op jit(solution)/shard_map/ppermute | solution.py:23
  265.7 6.4 %collective-permute-start.35 = (f32[1,16,32]{2,1,0:T(8,128)S(1)}, f32[1,16,32]{2,1,0:T(8,128)S(1)}, u32[]{:S(2)}, u32[]{:S(2)}) collective-permute-start(f32[1,16,32]{2,1,0:T(8,128)S(1)} %get-tuple-element.178), channel_id=1, source_target_pairs={{0,4},{4,8},{8,12},{12,16},{16,20},{20,24},{24,28},{1,5},{5,9},{9,... | collective-permute-start | bytes 6152 | tf_op jit(solution)/shard_map/ppermute | solution.py:23
  274.2 6.4 %collective-permute-start.37 = (f32[1,16,32]{2,1,0:T(8,128)S(1)}, f32[1,16,32]{2,1,0:T(8,128)S(1)}, u32[]{:S(2)}, u32[]{:S(2)}) collective-permute-start(f32[1,16,32]{2,1,0:T(8,128)S(1)} %get-tuple-element.172), channel_id=1, source_target_pairs={{0,4},{4,8},{8,12},{12,16},{16,20},{20,24},{24,28},{1,5},{5,9},{9,... | collective-permute-start | bytes 6152 | tf_op jit(solution)/shard_map/ppermute | solution.py:23
  282.8 6.4 %collective-permute-start.39 = (f32[1,16,32]{2,1,0:T(8,128)S(1)}, f32[1,16,32]{2,1,0:T(8,128)S(1)}, u32[]{:S(2)}, u32[]{:S(2)}) collective-permute-start(f32[1,16,32]{2,1,0:T(8,128)S(1)} %get-tuple-element.166), channel_id=1, source_target_pairs={{0,4},{4,8},{8,12},{12,16},{16,20},{20,24},{24,28},{1,5},{5,9},{9,... | collective-permute-start | bytes 6152 | tf_op jit(solution)/shard_map/ppermute | solution.py:23
  291.4 6.4 %collective-permute-start.41 = (f32[1,16,32]{2,1,0:T(8,128)S(1)}, f32[1,16,32]{2,1,0:T(8,128)S(1)}, u32[]{:S(2)}, u32[]{:S(2)}) collective-permute-start(f32[1,16,32]{2,1,0:T(8,128)S(1)} %get-tuple-element.160), channel_id=1, source_target_pairs={{0,4},{4,8},{8,12},{12,16},{16,20},{20,24},{24,28},{1,5},{5,9},{9,... | collective-permute-start | bytes 6152 | tf_op jit(solution)/shard_map/ppermute | solution.py:23
  300.1 6.4 %collective-permute-start.43 = (f32[1,16,32]{2,1,0:T(8,128)S(1)}, f32[1,16,32]{2,1,0:T(8,128)S(1)}, u32[]{:S(2)}, u32[]{:S(2)}) collective-permute-start(f32[1,16,32]{2,1,0:T(8,128)S(1)} %get-tuple-element.158), channel_id=1, source_target_pairs={{0,4},{4,8},{8,12},{12,16},{16,20},{20,24},{24,28},{1,5},{5,9},{9,... | collective-permute-start | bytes 6152 | tf_op jit(solution)/shard_map/ppermute | solution.py:23
  356.6 6.4 %collective-permute-start.56 = (f32[1,1,16,128]{3,2,1,0:T(8,128)S(1)}, f32[1,1,16,128]{3,2,1,0:T(8,128)S(1)}, u32[]{:S(2)}, u32[]{:S(2)}) collective-permute-start(f32[1,1,16,128]{3,2,1,0:T(8,128)S(1)} %get-tuple-element.102), channel_id=1, source_target_pairs={{0,4},{4,8},{8,12},{12,16},{16,20},{20,24},{24,28},{1,5},{5,9},{9,... | collective-permute-start | bytes 24584 | tf_op jit(solution)/shard_map/ppermute | solution.py:23
  372.4 6.4 %collective-permute-start.60 = (f32[1,1,16,128]{3,2,1,0:T(8,128)S(1)}, f32[1,1,16,128]{3,2,1,0:T(8,128)S(1)}, u32[]{:S(2)}, u32[]{:S(2)}) collective-permute-start(f32[1,1,16,128]{3,2,1,0:T(8,128)S(1)} %get-tuple-element.100), channel_id=1, source_target_pairs={{0,4},{4,8},{8,12},{12,16},{16,20},{20,24},{24,28},{1,5},{5,9},{9,... | collective-permute-start | bytes 24584 | tf_op jit(solution)/shard_map/ppermute | solution.py:23
  388.2 6.4 %collective-permute-start.64 = (f32[1,1,16,128]{3,2,1,0:T(8,128)S(1)}, f32[1,1,16,128]{3,2,1,0:T(8,128)S(1)}, u32[]{:S(2)}, u32[]{:S(2)}) collective-permute-start(f32[1,1,16,128]{3,2,1,0:T(8,128)S(1)} %get-tuple-element.98), channel_id=1, source_target_pairs={{0,4},{4,8},{8,12},{12,16},{16,20},{20,24},{24,28},{1,5},{5,9},{9,... | collective-permute-start | bytes 24584 | tf_op jit(solution)/shard_map/ppermute | solution.py:23
  (46 other events, 256.1 us)
where the time goes:
time: 405 us; the launch traced here: 403 us
  starting transfers between devices  181 us (45%)
  waiting for transfers between devices  85.1 us (21%)
  other arithmetic  69.4 us (17%)
  local copies, waits for them, and re-layouts  49.5 us (12%)
  blocking collectives  15.9 us (4%)
    ppermute x34, starting transfers between devices, padded_2(): lax.ppermute(tail, axis, [(i, (i + 1) % count) for i in range(ends)])  105 us
    ppermute x34, waiting for transfers between devices, padded_2(): lax.ppermute(tail, axis, [(i, (i + 1) % count) for i in range(ends)])  83 us
    ppermute x34, starting transfers between devices, padded_2(): lax.ppermute(head, axis, [((i + 1) % count, i) for i in range(ends)])  76.4 us
    reduce_sum x4, other arithmetic, coarsen(): return jnp.mean(split, axis=(-5, -3, -1))  36.5 us
    concatenate x1, local copies, waits for them, and re-layouts, padded_2(): jnp.concatenate([lax.ppermute(tail, axis, [(i, (i + 1) % count) for i in...  18.2 us
    another operation x3, other arithmetic, local_fields(): return jnp.stack([fields[0], fields[1], fields[2], storage])  16.5 us
    reshape x2, local copies, waits for them, and re-layouts, coarsen(): values.reshape(lead + (size_x // 2, 2, size_y // 2, 2, size_z // 2, 2))  10.9 us
    all_gather x1, blocking collectives, local(): lax.all_gather(narrow, 'gy', axis=2, tiled=True)  10.7 us
  transfers between devices with their start and end apart: 68, of which 33 were waited for; matrix products, arithmetic and copies ran while one was open for 15% of the time, Pallas kernels for 0%

commit v1 on v0

--- a/solution.py
+++ b/solution.py
@@ -1,7 +1,9 @@
+import functools
 import jax
 import jax.numpy as jnp
 from jax import lax
 from jax.sharding import PartitionSpec as P
+from jax.lax import axis_index, axis_size, ppermute
 
 CHEB = 3
 COARSE_SWEEPS = 8
@@ -10,6 +12,35 @@
 cheb_half = 0.9
 cheb_ratio = cheb_centre / cheb_half
 jacobi_weight = 0.8
+
+
+def touch_sheets_up(work_x, dim_at):
+    work_x = jnp.moveaxis(work_x, 0, dim_at)
+    w1 = work_x.shape
+    return work_x.reshape(*w1[:dim_at], w1[dim_at] * w1[dim_at + 1], *w1[dim_at + 2 :])
+
+
+def supply_run_on(s0, lane_axis):
+    f_now, field_out = (axis_size(lane_axis), axis_index(lane_axis))
+    g_now, value_now = (s0[None], 1)
+    while value_now < f_now:
+        slots = []
+        for k0 in range(f_now):
+            slots.append((k0, k0 ^ value_now))
+        current_block = ppermute(g_now, axis_name=lane_axis, perm=slots)
+        big = field_out & value_now == 0
+        g_now = jnp.concatenate(
+            [jnp.where(big, g_now, current_block), jnp.where(big, current_block, g_now)]
+        )
+        value_now *= 2
+    return g_now
+
+
+def step_on_stages_all_now(mine, xs, along_dim):
+    return touch_sheets_up(supply_run_on(mine, xs), along_dim)
+
+
+watch_skins_here = functools.partial(step_on_stages_all_now, xs="gy", along_dim=2)
 
 
 def padded_2(cells, sides, width):
@@ -172,7 +203,7 @@
     narrow = coarse_coeffs[:, :, 1:-1]
     group_source, group_coeffs = (
         lax.all_gather(coarse_source, "gy", axis=1, tiled=True),
-        lax.all_gather(narrow, "gy", axis=2, tiled=True),
+        watch_skins_here(narrow),
     )
     line_total = jnp.sum(group_source, axis=1)
     line_store = jnp.sum(group_coeffs[3, 1:-1], axis=1)

time: 405 us -> 392 us (0.968)
  blocking collectives: 15.9 us -> 5.19 us
    all_gather x1 -> x0, blocking collectives: 10.7 us -> none  [local(): lax.all_gather(narrow, 'gy', axis=2, tiled=True)]
    ppermute x34, starting transfers between devices: 76.4 us -> 72.1 us  [padded_2(): lax.ppermute(head, axis, [((i + 1) % count, i) for i in range(ends)])]
  transfers between devices with their start and end apart: 68 -> 70, of which waited for: 33 -> 34; matrix products, arithmetic and copies ran while one was open for 15% -> 15% of each run, Pallas kernels for 0% -> 0%
where the time goes in v1:
time: 392 us; the launch traced here: 389 us
  starting transfers between devices  179 us (46%)
  waiting for transfers between devices  87.4 us (22%)
  other arithmetic  68.7 us (18%)
  local copies, waits for them, and re-layouts  47.1 us (12%)
  blocking collectives  5.19 us (1%)
    ppermute x34, starting transfers between devices, padded_2(): lax.ppermute(tail, axis, [(i, (i + 1) % count) for i in range(ends)])  107 us
    ppermute x34, waiting for transfers between devices, padded_2(): lax.ppermute(tail, axis, [(i, (i + 1) % count) for i in range(ends)])  85.3 us
    ppermute x34, starting transfers between devices, padded_2(): lax.ppermute(head, axis, [((i + 1) % count, i) for i in range(ends)])  72.1 us
    reduce_sum x4, other arithmetic, coarsen(): return jnp.mean(split, axis=(-5, -3, -1))  36.6 us
    concatenate x1, local copies, waits for them, and re-layouts, padded_2(): jnp.concatenate([lax.ppermute(tail, axis, [(i, (i + 1) % count) for i in...  17.9 us
    another operation x3, other arithmetic, local_fields(): return jnp.stack([fields[0], fields[1], fields[2], storage])  16.1 us
    reshape x2, local copies, waits for them, and re-layouts, coarsen(): values.reshape(lead + (size_x // 2, 2, size_y // 2, 2, size_z // 2, 2))  10.8 us
    mul x1, other arithmetic, local_fields(): storage_scale * (1.0 + fields[3] * jnp.exp((fields[4] - 1.0) * jnp.log(co...  10.4 us
  transfers between devices with their start and end apart: 70, of which 34 were waited for; matrix products, arithmetic and copies ran while one was open for 15% of the time, Pallas kernels for 0%

profile of v1, /device:TPU:26, one launch (start us, length us, event | category | flops | bytes accessed | tf_op | source)
XLA Modules:
  0.0 389.3 jit_solution(14971885164743324348)
XLA Ops:
  5.5 6.0 %add_bitcast_fusion.3 = (f32[1,16,16,128]{3,2,1,0:T(8,128)S(1)}, pred[16,16,128]{2,1,0:T(8,128)(4,1)S(1)}, pred[16,16,128]{2,1,0:T(8,128)(4,1)S(1)}, pred[16,16,...) fusion(f32[]{:T(128)} %bitcast.23, f32[]{:T(128)} %bitcast.22, ...), kind=kLoop, calls=%fused_computation.161 | loop fusion | flops 753664 | bytes 524320 | tf_op jit(solution)/shard_map/stack | solution.py:184
  11.5 5.1 %add_bitcast_fusion.1 = f32[1,16,16,128]{3,2,1,0:T(8,128)S(1)} fusion(pred[16,16,128]{2,1,0:T(8,128)(4,1)S(1)} %get-tuple-element.44, pred[16,16,128]{2,1,0:T(8,128)(4,1)S(1)} %get-tuple-element.43, pred[16,16,128]{2,1,0:T(8,128)(4,1)S(1)} %get-tuple-element.42, pred[16,16,128]{2,1,0:T(8,128)(4,1)S(1)} %get-tuple-element.41, ...), kind=kLoop, calls=%fused_computation.159 | loop fusion | flops 491520 | bytes 393248 | tf_op jit(solution)/shard_map/stack | solution.py:184
  16.6 5.1 %add_bitcast_fusion.2 = f32[1,16,16,128]{3,2,1,0:T(8,128)S(1)} fusion(pred[16,16,128]{2,1,0:T(8,128)(4,1)S(1)} %get-tuple-element.44, pred[16,16,128]{2,1,0:T(8,128)(4,1)S(1)} %get-tuple-element.43, pred[16,16,128]{2,1,0:T(8,128)(4,1)S(1)} %get-tuple-element.42, pred[16,16,128]{2,1,0:T(8,128)(4,1)S(1)} %get-tuple-element.41, ...), kind=kLoop, calls=%fused_computation.160 | loop fusion | flops 491520 | bytes 393248 | tf_op jit(solution)/shard_map/stack | solution.py:184
  21.7 10.4 %add_multiply_fusion = f32[16,16,128]{2,1,0:T(8,128)S(1)} fusion(f32[16,16,128]{2,1,0:T(8,128)S(1)} %copy-done.1, pred[16,16,128]{2,1,0:T(8,128)(4,1)S(1)} %get-tuple-element.44, pred[16,16,128]{2,1,0:T(8,128)(4,1)S(1)} %get-tuple-element.43, pred[16,16,128]{2,1,0:T(8,128)(4,1)S(1)} %get-tuple-element.42, pred[16,16,128]{2,1,0:T(8,128)(4,1)S(1)} %get-tuple-element.41, ...), kind=kLoop, calls=%fused_computation.162 | loop fusion | flops 1146880 | bytes 524352 | tf_op jit(solution)/shard_map/mul | solution.py:183
  39.2 4.0 %collective-permute-done = f32[4,4,16,128]{3,2,1,0:T(8,128)S(1)} collective-permute-done((f32[4,4,16,128]{3,2,1,0:T(8,128)S(1)}, f32[4,4,16,128]{3,2,1,0:T(8,128)S(1)}, u32[]{:S(2)}, u32[]{:S(2)}) %collective-permute-start) | collective-permute-done | bytes 131104 | tf_op jit(solution)/shard_map/ppermute | solution.py:54
  59.4 17.9 %copy.584 = f32[4,24,24,128]{0,3,2,1:T(8,128)} copy(f32[4,24,24,128]{3,2,1,0:T(8,128)S(1)} %pad_maximum_fusion) | data formatting | bytes 2359296 | tf_op jit(solution)/shard_map/concatenate | solution.py:52
  77.4 27.0 %reduce_sum.55 = f32[4,12,12,64]{0,3,2,1:T(8,128)} reduce(f32[4,12,2,12,2,64,2]{0,6,5,4,3,2,1:T(2,128)} %bitcast.191, f32[]{:T(128)} %constant.27.clone.1), dimensions={2,4,6}, to_apply=%region_1.2 | reduce | flops 258048 | bytes 1327108 | tf_op jit(solution)/shard_map/reduce_sum | solution.py:116
  115.6 5.3 %reduce_sum.58 = f32[4,6,6,32]{0,3,2,1:T(8,128)S(1)} reduce(f32[4,6,2,6,2,32,2]{0,6,5,4,3,2,1:T(2,128)} %bitcast.192, f32[]{:T(128)} %constant.27.clone.1), dimensions={2,4,6}, to_apply=%region_4.5 | reduce | flops 32256 | bytes 165892 | tf_op jit(solution)/shard_map/reduce_sum | solution.py:116
  121.5 4.1 %collective-permute-start.9 = (f32[1,1,16,128]{3,2,1,0:T(8,128)S(1)}, f32[1,1,16,128]{3,2,1,0:T(8,128)S(1)}, u32[]{:S(2)}, u32[]{:S(2)}) collective-permute-start(f32[1,1,16,128]{3,2,1,0:T(8,128)S(1)} %get-tuple-element.109), channel_id=1, source_target_pairs={{4,0},{8,4},{12,8},{16,12},{20,16},{24,20},{28,24},{5,1},{9,5},{13... | collective-permute-start | bytes 24584 | tf_op jit(solution)/shard_map/ppermute | solution.py:56
  127.6 4.5 %collective-permute-done.8 = f32[1,1,16,128]{3,2,1,0:T(8,128)S(1)} collective-permute-done((f32[1,1,16,128]{3,2,1,0:T(8,128)S(1)}, f32[1,1,16,128]{3,2,1,0:T(8,128)S(1)}, u32[]{:S(2)}, u32[]{:S(2)}) %collective-permute-start.8) | collective-permute-done | bytes 8224 | tf_op jit(solution)/shard_map/ppermute | solution.py:54
  141.4 3.9 %collective-permute-start.12 = (f32[1,1,16,128]{3,2,1,0:T(8,128)S(1)}, f32[1,1,16,128]{3,2,1,0:T(8,128)S(1)}, u32[]{:S(2)}, u32[]{:S(2)}) collective-permute-start(f32[1,1,16,128]{3,2,1,0:T(8,128)S(1)} %get-tuple-element.106), channel_id=1, source_target_pairs={{0,4},{4,8},{8,12},{12,16},{16,20},{20,24},{24,28},{1,5},{5,9},{9,... | collective-permute-start | bytes 24584 | tf_op jit(solution)/shard_map/ppermute | solution.py:54
  155.3 9.8 %reshape.59 = f32[8,2,8,2,64,2]{5,4,3,2,1,0:T(8,128)} reshape(f32[16,16,128]{2,1,0:T(8,128)S(1)} %fusion.41) | data formatting | bytes 262144 | tf_op jit(solution)/shard_map/reshape | solution.py:115
  165.0 4.0 %reduce_sum.54 = f32[8,8,64]{2,1,0:T(8,128)S(1)} reduce(f32[8,2,8,2,64,2]{5,4,3,2,1,0:T(8,128)} %reshape.59, f32[]{:T(128)} %constant.27.clone.1), dimensions={1,3,5}, to_apply=%region_0.1 | reduce | flops 28672 | bytes 147460 | tf_op jit(solution)/shard_map/reduce_sum | solution.py:116
  187.6 3.9 %collective-permute-start.20 = (f32[1,1,8,64]{3,2,1,0:T(8,128)S(1)}, f32[1,1,8,64]{3,2,1,0:T(8,128)S(1)}, u32[]{:S(2)}, u32[]{:S(2)}) collective-permute-start(f32[1,1,8,64]{3,2,1,0:T(8,128)S(1)} %get-tuple-element.202), channel_id=1, source_target_pairs={{0,4},{4,8},{8,12},{12,16},{16,20},{20,24},{24,28},{1,5},{5,9},{9,... | collective-permute-start | bytes 6152 | tf_op jit(solution)/shard_map/ppermute | solution.py:54
  219.1 5.2 %all_gather.3 = f32[4,16,32]{2,0,1:T(4,128)S(1)} all-gather(f32[4,4,32]{2,0,1:T(4,128)S(1)} %copy.595), channel_id=1, replica_groups=mesh['gx'=8,'gy'=4] {'gy'}, dimensions={1}, use_global_device_ids=true | all-gather | bytes 10240 | tf_op jit(solution)/shard_map/all_gather | solution.py:205
  226.3 3.9 %collective-permute-start.31 = (f32[1,16,32]{2,1,0:T(8,128)S(1)}, f32[1,16,32]{2,1,0:T(8,128)S(1)}, u32[]{:S(2)}, u32[]{:S(2)}) collective-permute-start(f32[1,16,32]{2,1,0:T(8,128)S(1)} %broadcast_in_dim.289), channel_id=1, source_target_pairs={{0,4},{4,8},{8,12},{12,16},{16,20},{20,24},{24,28},{1,5},{5,9},{9,... | collective-permute-start | bytes 6152 | tf_op jit(solution)/shard_map/ppermute | solution.py:54
  235.1 3.9 %collective-permute-start.33 = (f32[1,16,32]{2,1,0:T(8,128)S(1)}, f32[1,16,32]{2,1,0:T(8,128)S(1)}, u32[]{:S(2)}, u32[]{:S(2)}) collective-permute-start(f32[1,16,32]{2,1,0:T(8,128)S(1)} %get-tuple-element.194), channel_id=1, source_target_pairs={{0,4},{4,8},{8,12},{12,16},{16,20},{20,24},{24,28},{1,5},{5,9},{9,... | collective-permute-start | bytes 6152 | tf_op jit(solution)/shard_map/ppermute | solution.py:54
  243.7 3.9 %collective-permute-start.35 = (f32[1,16,32]{2,1,0:T(8,128)S(1)}, f32[1,16,32]{2,1,0:T(8,128)S(1)}, u32[]{:S(2)}, u32[]{:S(2)}) collective-permute-start(f32[1,16,32]{2,1,0:T(8,128)S(1)} %get-tuple-element.188), channel_id=1, source_target_pairs={{0,4},{4,8},{8,12},{12,16},{16,20},{20,24},{24,28},{1,5},{5,9},{9,... | collective-permute-start | bytes 6152 | tf_op jit(solution)/shard_map/ppermute | solution.py:54
  252.2 3.9 %collective-permute-start.37 = (f32[1,16,32]{2,1,0:T(8,128)S(1)}, f32[1,16,32]{2,1,0:T(8,128)S(1)}, u32[]{:S(2)}, u32[]{:S(2)}) collective-permute-start(f32[1,16,32]{2,1,0:T(8,128)S(1)} %get-tuple-element.182), channel_id=1, source_target_pairs={{0,4},{4,8},{8,12},{12,16},{16,20},{20,24},{24,28},{1,5},{5,9},{9,... | collective-permute-start | bytes 6152 | tf_op jit(solution)/shard_map/ppermute | solution.py:54
  260.8 3.9 %collective-permute-start.39 = (f32[1,16,32]{2,1,0:T(8,128)S(1)}, f32[1,16,32]{2,1,0:T(8,128)S(1)}, u32[]{:S(2)}, u32[]{:S(2)}) collective-permute-start(f32[1,16,32]{2,1,0:T(8,128)S(1)} %get-tuple-element.176), channel_id=1, source_target_pairs={{0,4},{4,8},{8,12},{12,16},{16,20},{20,24},{24,28},{1,5},{5,9},{9,... | collective-permute-start | bytes 6152 | tf_op jit(solution)/shard_map/ppermute | solution.py:54
  269.4 3.9 %collective-permute-start.41 = (f32[1,16,32]{2,1,0:T(8,128)S(1)}, f32[1,16,32]{2,1,0:T(8,128)S(1)}, u32[]{:S(2)}, u32[]{:S(2)}) collective-permute-start(f32[1,16,32]{2,1,0:T(8,128)S(1)} %get-tuple-element.170), channel_id=1, source_target_pairs={{0,4},{4,8},{8,12},{12,16},{16,20},{20,24},{24,28},{1,5},{5,9},{9,... | collective-permute-start | bytes 6152 | tf_op jit(solution)/shard_map/ppermute | solution.py:54
  278.0 3.9 %collective-permute-start.43 = (f32[1,16,32]{2,1,0:T(8,128)S(1)}, f32[1,16,32]{2,1,0:T(8,128)S(1)}, u32[]{:S(2)}, u32[]{:S(2)}) collective-permute-start(f32[1,16,32]{2,1,0:T(8,128)S(1)} %get-tuple-element.164), channel_id=1, source_target_pairs={{0,4},{4,8},{8,12},{12,16},{16,20},{20,24},{24,28},{1,5},{5,9},{9,... | collective-permute-start | bytes 6152 | tf_op jit(solution)/shard_map/ppermute | solution.py:54
  326.7 3.9 %collective-permute-start.54 = (f32[1,1,8,64]{3,2,1,0:T(8,128)S(1)}, f32[1,1,8,64]{3,2,1,0:T(8,128)S(1)}, u32[]{:S(2)}, u32[]{:S(2)}) collective-permute-start(f32[1,1,8,64]{3,2,1,0:T(8,128)S(1)} %get-tuple-element.150), channel_id=1, source_target_pairs={{0,4},{4,8},{8,12},{12,16},{16,20},{20,24},{24,28},{1,5},{5,9},{9,... | collective-permute-start | bytes 6152 | tf_op jit(solution)/shard_map/ppermute | solution.py:54
  343.1 3.9 %collective-permute-start.58 = (f32[1,1,16,128]{3,2,1,0:T(8,128)S(1)}, f32[1,1,16,128]{3,2,1,0:T(8,128)S(1)}, u32[]{:S(2)}, u32[]{:S(2)}) collective-permute-start(f32[1,1,16,128]{3,2,1,0:T(8,128)S(1)} %get-tuple-element.104), channel_id=1, source_target_pairs={{0,4},{4,8},{8,12},{12,16},{16,20},{20,24},{24,28},{1,5},{5,9},{9,... | collective-permute-start | bytes 24584 | tf_op jit(solution)/shard_map/ppermute | solution.py:54
  (312 shorter events, 236.2 us)
Async XLA Ops:
  32.1 7.1 %collective-permute-start.1 = (f32[4,4,16,128]{3,2,1,0:T(8,128)S(1)}, f32[4,4,16,128]{3,2,1,0:T(8,128)S(1)}, u32[]{:S(2)}, u32[]{:S(2)}) collective-permute-start(f32[4,4,16,128]{3,2,1,0:T(8,128)S(1)} %get-tuple-element.51), channel_id=1, source_target_pairs={{4,0},{8,4},{12,8},{16,12},{20,16},{24,20},{28,24},{5,1},{9,5},{13... | collective-permute-start | bytes 393224 | tf_op jit(solution)/shard_map/ppermute | solution.py:56
  35.4 7.8 %collective-permute-start = (f32[4,4,16,128]{3,2,1,0:T(8,128)S(1)}, f32[4,4,16,128]{3,2,1,0:T(8,128)S(1)}, u32[]{:S(2)}, u32[]{:S(2)}) collective-permute-start(f32[4,4,16,128]{3,2,1,0:T(8,128)S(1)} %get-tuple-element.50), channel_id=1, source_target_pairs={{0,4},{4,8},{8,12},{12,16},{16,20},{20,24},{24,28},{1,5},{5,9},{9,... | collective-permute-start | bytes 393224 | tf_op jit(solution)/shard_map/ppermute | solution.py:54
  45.2 7.0 %collective-permute-start.2 = (f32[4,24,4,128]{3,1,2,0:T(8,128)S(1)}, f32[4,24,4,128]{3,1,2,0:T(8,128)S(1)}, u32[]{:S(2)}, u32[]{:S(2)}) collective-permute-start(f32[4,24,4,128]{3,1,2,0:T(8,128)S(1)} %copy.630), channel_id=1, source_target_pairs={{0,1},{1,2},{2,3},{4,5},{5,6},{6,7},{8,9},{9,10},{10,11},{12,13},{... | collective-permute-start | bytes 589832 | tf_op jit(solution)/shard_map/ppermute | solution.py:54
  53.6 54.6 %collective-permute-start.5 = (f32[1,1,16,128]{3,2,1,0:T(8,128)S(1)}, f32[1,1,16,128]{3,2,1,0:T(8,128)S(1)}, u32[]{:S(2)}, u32[]{:S(2)}) collective-permute-start(f32[1,1,16,128]{3,2,1,0:T(8,128)S(1)} %get-tuple-element.111), channel_id=1, source_target_pairs={{4,0},{8,4},{12,8},{16,12},{20,16},{24,20},{28,24},{5,1},{9,5},{13... | collective-permute-start | bytes 24584 | tf_op jit(solution)/shard_map/ppermute | solution.py:56
  56.8 51.4 %collective-permute-start.4 = (f32[1,1,16,128]{3,2,1,0:T(8,128)S(1)}, f32[1,1,16,128]{3,2,1,0:T(8,128)S(1)}, u32[]{:S(2)}, u32[]{:S(2)}) collective-permute-start(f32[1,1,16,128]{3,2,1,0:T(8,128)S(1)} %get-tuple-element.110), channel_id=1, source_target_pairs={{0,4},{4,8},{8,12},{12,16},{16,20},{20,24},{24,28},{1,5},{5,9},{9,... | collective-permute-start | bytes 24584 | tf_op jit(solution)/shard_map/ppermute | solution.py:54
  108.2 12.8 %collective-permute-start.7 = (f32[1,18,1,128]{3,2,1,0:T(1,128)S(1)}, f32[1,18,1,128]{3,2,1,0:T(1,128)S(1)}, u32[]{:S(2)}, u32[]{:S(2)}) collective-permute-start(f32[1,18,1,128]{3,2,1,0:T(1,128)S(1)} %get-tuple-element.99), channel_id=1, source_target_pairs={{1,0},{2,1},{3,2},{5,4},{6,5},{7,6},{9,8},{10,9},{11,10},{13,12},{... | collective-permute-start | bytes 27656 | tf_op jit(solution)/shard_map/ppermute | solution.py:56
  110.1 10.9 %collective-permute-start.6 = (f32[1,18,1,128]{3,2,1,0:T(1,128)S(1)}, f32[1,18,1,128]{3,2,1,0:T(1,128)S(1)}, u32[]{:S(2)}, u32[]{:S(2)}) collective-permute-start(f32[1,18,1,128]{3,2,1,0:T(1,128)S(1)} %get-tuple-element.98), channel_id=1, source_target_pairs={{0,1},{1,2},{2,3},{4,5},{5,6},{6,7},{8,9},{9,10},{10,11},{12,13},{... | collective-permute-start | bytes 27656 | tf_op jit(solution)/shard_map/ppermute | solution.py:54
  125.6 6.4 %collective-permute-start.8 = (f32[1,1,16,128]{3,2,1,0:T(8,128)S(1)}, f32[1,1,16,128]{3,2,1,0:T(8,128)S(1)}, u32[]{:S(2)}, u32[]{:S(2)}) collective-permute-start(f32[1,1,16,128]{3,2,1,0:T(8,128)S(1)} %get-tuple-element.108), channel_id=1, source_target_pairs={{0,4},{4,8},{8,12},{12,16},{16,20},{20,24},{24,28},{1,5},{5,9},{9,... | collective-permute-start | bytes 24584 | tf_op jit(solution)/shard_map/ppermute | solution.py:54
  141.4 6.4 %collective-permute-start.12 = (f32[1,1,16,128]{3,2,1,0:T(8,128)S(1)}, f32[1,1,16,128]{3,2,1,0:T(8,128)S(1)}, u32[]{:S(2)}, u32[]{:S(2)}) collective-permute-start(f32[1,1,16,128]{3,2,1,0:T(8,128)S(1)} %get-tuple-element.106), channel_id=1, source_target_pairs={{0,4},{4,8},{8,12},{12,16},{16,20},{20,24},{24,28},{1,5},{5,9},{9,... | collective-permute-start | bytes 24584 | tf_op jit(solution)/shard_map/ppermute | solution.py:54
  145.7 6.8 %collective-permute-start.28 = (f32[1,4,6,4,32]{4,3,2,1,0:T(4,128)S(1)}, f32[1,4,6,4,32]{4,3,2,1,0:T(4,128)S(1)}, u32[]{:S(2)}, u32[]{:S(2)}) collective-permute-start(f32[1,4,6,4,32]{4,3,2,1,0:T(4,128)S(1)} %bitcast.241), channel_id=1, source_target_pairs={{0,1},{1,0},{2,3},{3,2},{4,5},{5,4},{6,7},{7,6},{8,9},{9,8},{10,11... | collective-permute-start | bytes 36872 | tf_op jit(solution)/shard_map/ppermute | solution.py:30
  172.1 6.4 %collective-permute-start.16 = (f32[1,1,8,64]{3,2,1,0:T(8,128)S(1)}, f32[1,1,8,64]{3,2,1,0:T(8,128)S(1)}, u32[]{:S(2)}, u32[]{:S(2)}) collective-permute-start(f32[1,1,8,64]{3,2,1,0:T(8,128)S(1)} %get-tuple-element.204), channel_id=1, source_target_pairs={{0,4},{4,8},{8,12},{12,16},{16,20},{20,24},{24,28},{1,5},{5,9},{9,... | collective-permute-start | bytes 6152 | tf_op jit(solution)/shard_map/ppermute | solution.py:54
  175.1 7.8 %collective-permute-start.29 = (f32[2,4,6,4,32]{4,3,2,1,0:T(4,128)S(1)}, f32[2,4,6,4,32]{4,3,2,1,0:T(4,128)S(1)}, u32[]{:S(2)}, u32[]{:S(2)}) collective-permute-start(f32[2,4,6,4,32]{4,3,2,1,0:T(4,128)S(1)} %pad_maximum_fusion.11), channel_id=1, source_target_pairs={{0,2},{1,3},{2,0},{3,1},{4,6},{5,7},{6,4},{7,5},{8,10},{9,11},{10,... | collective-permute-start | bytes 73736 | tf_op jit(solution)/shard_map/ppermute | solution.py:30
  187.6 6.4 %collective-permute-start.20 = (f32[1,1,8,64]{3,2,1,0:T(8,128)S(1)}, f32[1,1,8,64]{3,2,1,0:T(8,128)S(1)}, u32[]{:S(2)}, u32[]{:S(2)}) collective-permute-start(f32[1,1,8,64]{3,2,1,0:T(8,128)S(1)} %get-tuple-element.202), channel_id=1, source_target_pairs={{0,4},{4,8},{8,12},{12,16},{16,20},{20,24},{24,28},{1,5},{5,9},{9,... | collective-permute-start | bytes 6152 | tf_op jit(solution)/shard_map/ppermute | solution.py:54
  226.3 6.4 %collective-permute-start.31 = (f32[1,16,32]{2,1,0:T(8,128)S(1)}, f32[1,16,32]{2,1,0:T(8,128)S(1)}, u32[]{:S(2)}, u32[]{:S(2)}) collective-permute-start(f32[1,16,32]{2,1,0:T(8,128)S(1)} %broadcast_in_dim.289), channel_id=1, source_target_pairs={{0,4},{4,8},{8,12},{12,16},{16,20},{20,24},{24,28},{1,5},{5,9},{9,... | collective-permute-start | bytes 6152 | tf_op jit(solution)/shard_map/ppermute | solution.py:54
  235.1 6.4 %collective-permute-start.33 = (f32[1,16,32]{2,1,0:T(8,128)S(1)}, f32[1,16,32]{2,1,0:T(8,128)S(1)}, u32[]{:S(2)}, u32[]{:S(2)}) collective-permute-start(f32[1,16,32]{2,1,0:T(8,128)S(1)} %get-tuple-element.194), channel_id=1, source_target_pairs={{0,4},{4,8},{8,12},{12,16},{16,20},{20,24},{24,28},{1,5},{5,9},{9,... | collective-permute-start | bytes 6152 | tf_op jit(solution)/shard_map/ppermute | solution.py:54
  243.7 6.4 %collective-permute-start.35 = (f32[1,16,32]{2,1,0:T(8,128)S(1)}, f32[1,16,32]{2,1,0:T(8,128)S(1)}, u32[]{:S(2)}, u32[]{:S(2)}) collective-permute-start(f32[1,16,32]{2,1,0:T(8,128)S(1)} %get-tuple-element.188), channel_id=1, source_target_pairs={{0,4},{4,8},{8,12},{12,16},{16,20},{20,24},{24,28},{1,5},{5,9},{9,... | collective-permute-start | bytes 6152 | tf_op jit(solution)/shard_map/ppermute | solution.py:54
  252.2 6.4 %collective-permute-start.37 = (f32[1,16,32]{2,1,0:T(8,128)S(1)}, f32[1,16,32]{2,1,0:T(8,128)S(1)}, u32[]{:S(2)}, u32[]{:S(2)}) collective-permute-start(f32[1,16,32]{2,1,0:T(8,128)S(1)} %get-tuple-element.182), channel_id=1, source_target_pairs={{0,4},{4,8},{8,12},{12,16},{16,20},{20,24},{24,28},{1,5},{5,9},{9,... | collective-permute-start | bytes 6152 | tf_op jit(solution)/shard_map/ppermute | solution.py:54
  260.8 6.4 %collective-permute-start.39 = (f32[1,16,32]{2,1,0:T(8,128)S(1)}, f32[1,16,32]{2,1,0:T(8,128)S(1)}, u32[]{:S(2)}, u32[]{:S(2)}) collective-permute-start(f32[1,16,32]{2,1,0:T(8,128)S(1)} %get-tuple-element.176), channel_id=1, source_target_pairs={{0,4},{4,8},{8,12},{12,16},{16,20},{20,24},{24,28},{1,5},{5,9},{9,... | collective-permute-start | bytes 6152 | tf_op jit(solution)/shard_map/ppermute | solution.py:54
  269.4 6.4 %collective-permute-start.41 = (f32[1,16,32]{2,1,0:T(8,128)S(1)}, f32[1,16,32]{2,1,0:T(8,128)S(1)}, u32[]{:S(2)}, u32[]{:S(2)}) collective-permute-start(f32[1,16,32]{2,1,0:T(8,128)S(1)} %get-tuple-element.170), channel_id=1, source_target_pairs={{0,4},{4,8},{8,12},{12,16},{16,20},{20,24},{24,28},{1,5},{5,9},{9,... | collective-permute-start | bytes 6152 | tf_op jit(solution)/shard_map/ppermute | solution.py:54
  278.0 6.5 %collective-permute-start.43 = (f32[1,16,32]{2,1,0:T(8,128)S(1)}, f32[1,16,32]{2,1,0:T(8,128)S(1)}, u32[]{:S(2)}, u32[]{:S(2)}) collective-permute-start(f32[1,16,32]{2,1,0:T(8,128)S(1)} %get-tuple-element.164), channel_id=1, source_target_pairs={{0,4},{4,8},{8,12},{12,16},{16,20},{20,24},{24,28},{1,5},{5,9},{9,... | collective-permute-start | bytes 6152 | tf_op jit(solution)/shard_map/ppermute | solution.py:54
  286.7 6.4 %collective-permute-start.45 = (f32[1,16,32]{2,1,0:T(8,128)S(1)}, f32[1,16,32]{2,1,0:T(8,128)S(1)}, u32[]{:S(2)}, u32[]{:S(2)}) collective-permute-start(f32[1,16,32]{2,1,0:T(8,128)S(1)} %get-tuple-element.162), channel_id=1, source_target_pairs={{0,4},{4,8},{8,12},{12,16},{16,20},{20,24},{24,28},{1,5},{5,9},{9,... | collective-permute-start | bytes 6152 | tf_op jit(solution)/shard_map/ppermute | solution.py:54
  343.1 6.4 %collective-permute-start.58 = (f32[1,1,16,128]{3,2,1,0:T(8,128)S(1)}, f32[1,1,16,128]{3,2,1,0:T(8,128)S(1)}, u32[]{:S(2)}, u32[]{:S(2)}) collective-permute-start(f32[1,1,16,128]{3,2,1,0:T(8,128)S(1)} %get-tuple-element.104), channel_id=1, source_target_pairs={{0,4},{4,8},{8,12},{12,16},{16,20},{20,24},{24,28},{1,5},{5,9},{9,... | collective-permute-start | bytes 24584 | tf_op jit(solution)/shard_map/ppermute | solution.py:54
  358.9 6.4 %collective-permute-start.62 = (f32[1,1,16,128]{3,2,1,0:T(8,128)S(1)}, f32[1,1,16,128]{3,2,1,0:T(8,128)S(1)}, u32[]{:S(2)}, u32[]{:S(2)}) collective-permute-start(f32[1,1,16,128]{3,2,1,0:T(8,128)S(1)} %get-tuple-element.102), channel_id=1, source_target_pairs={{0,4},{4,8},{8,12},{12,16},{16,20},{20,24},{24,28},{1,5},{5,9},{9,... | collective-permute-start | bytes 24584 | tf_op jit(solution)/shard_map/ppermute | solution.py:54
  374.7 6.4 %collective-permute-start.66 = (f32[1,1,16,128]{3,2,1,0:T(8,128)S(1)}, f32[1,1,16,128]{3,2,1,0:T(8,128)S(1)}, u32[]{:S(2)}, u32[]{:S(2)}) collective-permute-start(f32[1,1,16,128]{3,2,1,0:T(8,128)S(1)} %get-tuple-element.100), channel_id=1, source_target_pairs={{0,4},{4,8},{8,12},{12,16},{16,20},{20,24},{24,28},{1,5},{5,9},{9,... | collective-permute-start | bytes 24584 | tf_op jit(solution)/shard_map/ppermute | solution.py:54
  (48 other events, 268.8 us)
